TPU v7x, 512 devices: a whole 4x8x8 slice. The times are simulated.
512 devices in a mesh: col: 8 (over z), tile: 64 (over y, x, core).
Axes of the slice: x: 4, y: 8, z: 8, core: 2. Of those that a mesh axis runs over, the one named last changes fastest.
Arguments:
- panel_factor: bfloat16 [8, 64, 2, 512, 512], P('col', 'tile'), may hold values from -0.15625 to 0.15625
- panel_cotangent: bfloat16 [8, 64, 2, 512, 512], P('col', 'tile'), may hold values from -1.5 to 1.5
- diag_factor: bfloat16 [8, 512, 512], P('col'), as said below
- diag_inverse: bfloat16 [8, 512, 512], P('col'), as said below
- diag_cotangent: float32 [8, 512, 512], P('col', 'tile'), may hold values from -6 to 6
- tile_count: int32 [8, 64], P('col', 'tile'), may hold values from 1 to 2, as said below
- tile_rows: int32 [8, 64, 2], P('col', 'tile'), may hold values from 1 to 255, as said below
Outputs:
- panel_adjoint: bfloat16 [8, 64, 2, 512, 512], P('col', 'tile')
- diag_adjoint: float32 [8, 512, 512], P('col', 'tile')
Inputs may be any that keep to these rules, and one draw needn't show every extreme that they name: `tile_count`: every device holds 1 to 2 live tiles of each panel column, in its first slots; in every column some device holds 2. `tile_rows`: in column c the live slots name distinct block rows; exactly one live slot names row c + 1, every other slot names a row of c + 2 or more. `diag_factor`: lower triangular with diagonal entries between 0.8 and 1.6. `diag_inverse`: lower triangular with diagonal entries between 0.8 and 1.6.
All inputs are finite; a program needn't handle non-finite values.
Results may differ from a plain program's by a relative error of at most 0.0044.
Values sent between devices are 32-bit elements; how exact they have to be, the bound alone decides.
No kernel may reach another device: no remote copies, remote signals or barrier semaphores. Data moves between devices by JAX's collectives and lax.ppermute only.
A program may use at most 128 MiB of HBM per device.

v0:
```python
import jax
import jax.numpy as jnp
from jax import lax
from jax.sharding import PartitionSpec as P


def passed_along(value, axis, by):
    count = lax.axis_size(axis)
    pairs = [(i, i + by) for i in range(count) if 0 <= i + by < count]
    return lax.ppermute(value, axis, pairs)


def symmetrize(matrix):
    strict = jnp.tril(matrix, -1)
    return strict + strict.T + jnp.diag(jnp.diagonal(matrix))


def on_device(
    panel_factor, panel_cotangent, diag_factor, diag_inverse, diag_cotangent, tile_count, tile_rows
):
    full = lax.Precision.HIGHEST
    factors = panel_factor[0, 0]
    cotangent = panel_cotangent[0, 0]
    lower = diag_factor[0]
    inverse = diag_inverse[0]
    width = lower.shape[0]
    rows_dev = diag_cotangent.shape[1]
    slot_count = factors.shape[0]
    column = lax.axis_index("col")
    groups = lax.axis_size("col")
    row_start = lax.axis_index("tile") * rows_dev
    live_slot = jnp.arange(slot_count) < tile_count[0, 0]
    link_flag = live_slot & (tile_rows[0, 0] == column + 1)
    solved = jnp.einsum("sij,jk->sik", cotangent, inverse, preferred_element_type=jnp.float32)
    rounded = jnp.where(
        live_slot[:, None, None], solved.astype(jnp.bfloat16), jnp.zeros_like(cotangent)
    )
    panel_terms = -jnp.einsum("sij,sik->jk", rounded, factors, preferred_element_type=jnp.float32)
    own_rows = lax.dynamic_slice_in_dim(panel_terms, row_start, rows_dev, 0) + diag_cotangent[0]
    panel_terms = lax.dynamic_update_slice_in_dim(panel_terms, own_rows, row_start, 0)
    chosen = jnp.sum(jnp.where(link_flag[:, None, None], factors, jnp.zeros_like(factors)), axis=0)
    link_part = jnp.dot(chosen, inverse, preferred_element_type=jnp.float32)
    summed, link_wide = lax.psum((panel_terms, link_part), "tile")
    inverse_wide = inverse.astype(jnp.float32)
    curvature = jnp.dot(lower.astype(jnp.float32).T, summed, precision=full)
    symmetric = symmetrize(curvature)
    own_map = 0.5 * jnp.dot(
        inverse_wide.T, jnp.dot(symmetric, inverse_wide, precision=full), precision=full
    )
    own_cols = lax.dynamic_slice_in_dim(own_map, row_start, rows_dev, 1)
    link_cols = lax.dynamic_slice_in_dim(link_wide, row_start, rows_dev, 1)
    incoming = jnp.zeros((width, width), jnp.float32)
    for sweep in range(groups - 1):
        advanced = own_cols + jnp.dot(
            link_wide.T, jnp.dot(incoming, link_cols, precision=full), precision=full
        )
        arrived = passed_along(advanced, "col", -1)
        incoming = lax.all_gather(arrived, "tile", axis=1, tiled=True)
    product = jnp.dot(incoming, link_wide, precision=full)
    link_rows = lax.dynamic_slice_in_dim(link_wide, row_start, rows_dev, 1)
    own_part = lax.dynamic_slice_in_dim(own_map, row_start, rows_dev, 0)
    diag_rows = own_part + jnp.dot(link_rows.T, product, precision=full)
    adjusted = (solved - 2.0 * product[None]).astype(jnp.bfloat16)
    panel_out = jnp.where(link_flag[:, None, None], adjusted, rounded)
    return (panel_out[None, None], diag_rows[None])


def solution(mesh):
    in_specs = (
        P("col", "tile", None, None, None),
        P("col", "tile", None, None, None),
        P("col", None, None),
        P("col", None, None),
        P("col", "tile", None),
        P("col", "tile"),
        P("col", "tile", None),
    )
    out_specs = (P("col", "tile", None, None, None), P("col", "tile", None))
    return jax.shard_map(
        on_device, mesh=mesh, in_specs=in_specs, out_specs=out_specs, check_vma=False
    )
```

profile of v0, /device:TPU:1, one launch (start us, length us, event | category | flops | bytes accessed | tf_op | source)
XLA Modules:
  0.0 887.5 jit_solution(10775126027155299674)
XLA Ops:
  18.6 204.7 %all-reduce.3.cloned.1.call-done = (f32[512,512]{1,0:T(8,128)}, f32[512,512]{1,0:T(8,128)}) async-done(((f32[512,512]{1,0:T(8,128)}, f32[512,512]{1,0:T(8,128)}), (f32[512,512]{1,0:T(8,128)}, f32[512,512]{1,0:T(8,128)})) %all-reduce.3.cloned.1.call-update) | async-done | bytes 2097168 | tf_op jit(solution)/shard_map/psum | solution.py:43
  224.5 3.2 fusion.15
  229.3 4.5 gather_fusion
  239.5 3.2 collective-permute-done
  243.3 84.6 %all-gather.8.cloned.1.call-done = f32[512,512]{0,1:T(8,128)} async-done(((f32[512,8]{0,1:T(8,128)}), f32[512,512]{0,1:T(8,128)}) %all-gather.8.cloned.1.call-update) | async-done | bytes 1048592 | tf_op jit(solution)/shard_map/all_gather | solution.py:58
  327.9 3.1 fusion.38
  333.1 3.2 collective-permute-done.1
  336.9 81.4 %all-gather.10.cloned.1.call-done = f32[512,512]{0,1:T(8,128)} async-done(((f32[512,8]{0,1:T(8,128)}), f32[512,512]{0,1:T(8,128)}) %all-gather.10.cloned.1.call-update) | async-done | bytes 1048592 | tf_op jit(solution)/shard_map/all_gather | solution.py:58
  418.3 3.1 fusion.36
  423.4 3.2 collective-permute-done.2
  427.5 81.2 %all-gather.12.cloned.1.call-done = f32[512,512]{0,1:T(8,128)} async-done(((f32[512,8]{0,1:T(8,128)}), f32[512,512]{0,1:T(8,128)}) %all-gather.12.cloned.1.call-update) | async-done | bytes 1048592 | tf_op jit(solution)/shard_map/all_gather | solution.py:58
  508.6 3.1 fusion.34
  513.8 3.2 collective-permute-done.3
  517.6 81.4 %all-gather.14.cloned.1.call-done = f32[512,512]{0,1:T(8,128)} async-done(((f32[512,8]{0,1:T(8,128)}), f32[512,512]{0,1:T(8,128)}) %all-gather.14.cloned.1.call-update) | async-done | bytes 1048592 | tf_op jit(solution)/shard_map/all_gather | solution.py:58
  599.0 3.1 fusion.32
  604.1 3.2 collective-permute-done.4
  608.0 81.4 %all-gather.16.cloned.1.call-done = f32[512,512]{0,1:T(8,128)} async-done(((f32[512,8]{0,1:T(8,128)}), f32[512,512]{0,1:T(8,128)}) %all-gather.16.cloned.1.call-update) | async-done | bytes 1048592 | tf_op jit(solution)/shard_map/all_gather | solution.py:58
  689.3 3.1 fusion.30
  694.5 3.2 collective-permute-done.5
  698.3 81.4 %all-gather.18.cloned.1.call-done = f32[512,512]{0,1:T(8,128)} async-done(((f32[512,8]{0,1:T(8,128)}), f32[512,512]{0,1:T(8,128)}) %all-gather.18.cloned.1.call-update) | async-done | bytes 1048592 | tf_op jit(solution)/shard_map/all_gather | solution.py:58
  779.7 3.1 fusion.28
  788.6 81.4 %all-gather.20.cloned.1.call-done = f32[512,512]{0,1:T(8,128)} async-done(((f32[512,8]{0,1:T(8,128)}), f32[512,512]{0,1:T(8,128)}) %all-gather.20.cloned.1.call-update) | async-done | bytes 1048592 | tf_op jit(solution)/shard_map/all_gather | solution.py:58
  870.0 3.1 broadcast_multiply_fusion
  876.7 3.9 fusion.3
  (75 shorter events, 42.4 us)
Async XLA Ops:
  7.2 5.5 copy-start
  7.2 5.5 copy-start.2
  7.2 216.2 %all-reduce.3.cloned.1.call-start = ((), (), s32[]{:S(2)}) async-start(), calls=%async_computation.7 | async-start | bytes 4194304 | tf_op jit(solution)/shard_map/psum | solution.py:43
  14.8 2.7 copy-start.7
  17.5 207.0 %copy-start.6 = (bf16[1,512,512]{2,1,0:T(8,128)(2,1)S(1)}, bf16[1,512,512]{2,1,0:T(8,128)(2,1)}, u32[]{:S(2)}) copy-start(bf16[1,512,512]{2,1,0:T(8,128)(2,1)} %param.9) | copy-start | bytes 1572868
  17.5 1.0 copy-start.5
  18.5 309.4 %all-gather.8.cloned.1.call-start = ((), (), s32[]{:S(2)}) async-start(), calls=%async_computation | async-start | bytes 1064960 | tf_op jit(solution)/shard_map/all_gather | solution.py:58
  233.8 2.5 copy-start.3
  236.3 1.2 copy-start.1
  237.5 545.3 %copy-start.4 = (f32[512,512]{1,0:T(8,128)}, f32[512,512]{1,0:T(8,128)S(1)}, u32[]{:S(2)}) copy-start(f32[512,512]{1,0:T(8,128)S(1)} %convolution_multiply_fusion) | copy-start | bytes 3145732
  238.2 4.5 collective-permute-start
  243.3 175.0 %all-gather.10.cloned.1.call-start = ((), (), s32[]{:S(2)}) async-start(), calls=%async_computation.1 | async-start | bytes 1064960 | tf_op jit(solution)/shard_map/all_gather | solution.py:58
  331.8 4.5 collective-permute-start.1
  336.9 171.8 %all-gather.12.cloned.1.call-start = ((), (), s32[]{:S(2)}) async-start(), calls=%async_computation.2 | async-start | bytes 1064960 | tf_op jit(solution)/shard_map/all_gather | solution.py:58
  422.1 4.5 collective-permute-start.2
  427.2 171.8 %all-gather.14.cloned.1.call-start = ((), (), s32[]{:S(2)}) async-start(), calls=%async_computation.3 | async-start | bytes 1064960 | tf_op jit(solution)/shard_map/all_gather | solution.py:58
  512.5 4.5 collective-permute-start.3
  517.6 171.8 %all-gather.16.cloned.1.call-start = ((), (), s32[]{:S(2)}) async-start(), calls=%async_computation.4 | async-start | bytes 1064960 | tf_op jit(solution)/shard_map/all_gather | solution.py:58
  602.8 4.5 collective-permute-start.4
  607.9 171.8 %all-gather.18.cloned.1.call-start = ((), (), s32[]{:S(2)}) async-start(), calls=%async_computation.5 | async-start | bytes 1064960 | tf_op jit(solution)/shard_map/all_gather | solution.py:58
  693.2 4.5 collective-permute-start.5
  698.3 171.8 %all-gather.20.cloned.1.call-start = ((), (), s32[]{:S(2)}) async-start(), calls=%async_computation.6 | async-start | bytes 1064960 | tf_op jit(solution)/shard_map/all_gather | solution.py:58
  783.5 4.5 collective-permute-start.6
  788.0 0.6 copy-start.14
  (6 other events, 3.6 us)
Sparse Core Ops, SparseCore 0:
  18.7 204.6 all-reduce.2
  243.4 84.4 all-gather.7
  337.0 81.2 all-gather.9
  427.3 81.2 all-gather.11
  517.7 81.2 all-gather.13
  608.0 81.2 all-gather.15
  698.4 81.2 all-gather.17
  788.8 81.2 all-gather.19
where the time goes:
time: 888 us; the launch traced here: 887 us
  waiting for transfers between devices  799 us (90%)
  matrix products  43.5 us (5%)
  between operations  15.2 us (2%)
  local copies, waits for them, and re-layouts  12.2 us (1%)
  starting transfers between devices  9.75 us (1%)
    all_gather x7, waiting for transfers between devices, on_device(): incoming = lax.all_gather(arrived, 'tile', axis=1, tiled=True)  573 us
    psum x1, waiting for transfers between devices, on_device(): summed, link_wide = lax.psum((panel_terms, link_part), 'tile')  205 us
    ppermute x7, waiting for transfers between devices, passed_along(): return lax.ppermute(value, axis, pairs)  22.1 us
    dot_general x6, matrix products, on_device(): jnp.dot(incoming, link_cols, precision=full)  18.8 us
  transfers between devices with their start and end apart: 15, of which 15 were waited for; matrix products, arithmetic and copies ran while one was open for 0% of the time, Pallas kernels for 0%

commit v1 on v0

--- a/solution.py
+++ b/solution.py
@@ -55,7 +55,9 @@
             link_wide.T, jnp.dot(incoming, link_cols, precision=full), precision=full
         )
         arrived = passed_along(advanced, "col", -1)
-        incoming = lax.all_gather(arrived, "tile", axis=1, tiled=True)
+        incoming = jnp.concatenate(
+            lax.all_to_all(jnp.stack([arrived] * lax.axis_size("tile")), "tile", 0, 0), axis=1
+        )
     product = jnp.dot(incoming, link_wide, precision=full)
     link_rows = lax.dynamic_slice_in_dim(link_wide, row_start, rows_dev, 1)
     own_part = lax.dynamic_slice_in_dim(own_map, row_start, rows_dev, 0)

time: 888 us -> 565 us (0.64)
  waiting for transfers between devices: 799 us -> 232 us
  blocking collectives: 0 us -> 250 us
    all_gather x7 -> x0, waiting for transfers between devices: 573 us -> none  [on_device(): incoming = lax.all_gather(arrived, 'tile', axis=1, tiled=True)]
    all_to_all x0 -> x7, blocking collectives: none -> 250 us  [on_device(): lax.all_to_all(jnp.stack([arrived] * lax.axis_size('tile')), 'tile', 0, 0)]
  transfers between devices with their start and end apart: 15 -> 8, of which waited for: 15 -> 8; matrix products, arithmetic and copies ran while one was open for 0% -> 0% of each run, Pallas kernels for 0% -> 0%
where the time goes in v1:
time: 565 us; the launch traced here: 562 us
  blocking collectives  250 us (44%)
  waiting for transfers between devices  232 us (41%)
  matrix products  40.2 us (7%)
  between operations  15 us (3%)
  starting transfers between devices  9.06 us (2%)
  local copies, waits for them, and re-layouts  7.83 us (1%)
  other arithmetic  7.52 us (1%)
    all_to_all x7, blocking collectives, on_device(): lax.all_to_all(jnp.stack([arrived] * lax.axis_size('tile')), 'tile', 0, 0)  250 us
    psum x1, waiting for transfers between devices, on_device(): summed, link_wide = lax.psum((panel_terms, link_part), 'tile')  205 us
    ppermute x7, waiting for transfers between devices, passed_along(): return lax.ppermute(value, axis, pairs)  27.1 us
    dot_general x6, matrix products, on_device(): jnp.dot(incoming, link_cols, precision=full)  11.5 us
  transfers between devices with their start and end apart: 8, of which 8 were waited for; matrix products, arithmetic and copies ran while one was open for 0% of the time, Pallas kernels for 0%

profile of v1, /device:TPU:1, one launch (start us, length us, event | category | flops | bytes accessed | tf_op | source)
XLA Modules:
  0.0 561.9 jit_solution(5562442708454797229)
XLA Ops:
  10.3 2.5 fusion.34
  13.5 3.8 fusion
  18.6 204.7 %all-reduce.3.cloned.1.call-done = (f32[512,512]{1,0:T(8,128)}, f32[512,512]{1,0:T(8,128)}) async-done(((f32[512,512]{1,0:T(8,128)}, f32[512,512]{1,0:T(8,128)}), (f32[512,512]{1,0:T(8,128)}, f32[512,512]{1,0:T(8,128)})) %all-reduce.3.cloned.1.call-update) | async-done | bytes 2097168 | tf_op jit(solution)/shard_map/psum | solution.py:43
  224.4 3.3 fusion.29
  229.3 4.5 gather_fusion
  233.9 2.4 fusion.22
  239.5 3.2 collective-permute-done
  242.8 39.2 %all_to_all.35 = f32[64,512,8]{1,2,0:T(8,128)S(1)} all-to-all(f32[64,512,8]{1,2,0:T(8,128)S(1)} %stack.14), channel_id=1, replica_groups=mesh['col'=8,'tile'=64] {'tile'}, dimensions={0} | all-to-all | bytes 2097152 | tf_op jit(solution)/shard_map/all_to_all | solution.py:59
  286.6 3.2 collective-permute-done.1
  289.9 35.4 %all_to_all.36 = f32[64,512,8]{1,2,0:T(8,128)S(1)} all-to-all(f32[64,512,8]{1,2,0:T(8,128)S(1)} %stack.15), channel_id=1, replica_groups=mesh['col'=8,'tile'=64] {'tile'}, dimensions={0} | all-to-all | bytes 2097152 | tf_op jit(solution)/shard_map/all_to_all | solution.py:59
  329.9 3.2 collective-permute-done.2
  333.2 35.4 %all_to_all.37 = f32[64,512,8]{1,2,0:T(8,128)S(1)} all-to-all(f32[64,512,8]{1,2,0:T(8,128)S(1)} %stack.16), channel_id=1, replica_groups=mesh['col'=8,'tile'=64] {'tile'}, dimensions={0} | all-to-all | bytes 2097152 | tf_op jit(solution)/shard_map/all_to_all | solution.py:59
  373.3 3.6 collective-permute-done.3
  377.0 35.1 %all_to_all.38 = f32[64,512,8]{1,2,0:T(8,128)S(1)} all-to-all(f32[64,512,8]{1,2,0:T(8,128)S(1)} %stack.17), channel_id=1, replica_groups=mesh['col'=8,'tile'=64] {'tile'}, dimensions={0} | all-to-all | bytes 2097152 | tf_op jit(solution)/shard_map/all_to_all | solution.py:59
  416.7 4.7 collective-permute-done.4
  421.5 35.1 %all_to_all.39 = f32[64,512,8]{1,2,0:T(8,128)S(1)} all-to-all(f32[64,512,8]{1,2,0:T(8,128)S(1)} %stack.18), channel_id=1, replica_groups=mesh['col'=8,'tile'=64] {'tile'}, dimensions={0} | all-to-all | bytes 2097152 | tf_op jit(solution)/shard_map/all_to_all | solution.py:59
  456.6 1.9 fusion.8
  461.3 4.7 collective-permute-done.5
  466.1 35.1 %all_to_all.40 = f32[64,512,8]{1,2,0:T(8,128)S(1)} all-to-all(f32[64,512,8]{1,2,0:T(8,128)S(1)} %stack.19), channel_id=1, replica_groups=mesh['col'=8,'tile'=64] {'tile'}, dimensions={0} | all-to-all | bytes 2097152 | tf_op jit(solution)/shard_map/all_to_all | solution.py:59
  505.9 4.7 collective-permute-done.6
  510.6 35.1 %all_to_all.41 = f32[64,512,8]{1,2,0:T(8,128)S(1)} all-to-all(f32[64,512,8]{1,2,0:T(8,128)S(1)} %stack.20), channel_id=1, replica_groups=mesh['col'=8,'tile'=64] {'tile'}, dimensions={0} | all-to-all | bytes 2097152 | tf_op jit(solution)/shard_map/all_to_all | solution.py:59
  545.8 2.8 broadcast_multiply_fusion
  548.6 3.0 fusion.1
  552.3 2.8 fusion.3
  (56 shorter events, 37.7 us)
Async XLA Ops:
  7.2 5.6 copy-start
  7.2 216.1 %all-reduce.3.cloned.1.call-start = ((), (), s32[]{:S(2)}) async-start(), calls=%async_computation.7 | async-start | bytes 4194304 | tf_op jit(solution)/shard_map/psum | solution.py:43
  8.0 4.8 copy-start.4
  13.4 3.8 copy-start.2
  13.5 3.8 copy-start.8
  18.6 205.9 %copy-start.7 = (bf16[1,512,512]{2,1,0:T(8,128)(2,1)S(1)}, bf16[1,512,512]{2,1,0:T(8,128)(2,1)}, u32[]{:S(2)}) copy-start(bf16[1,512,512]{2,1,0:T(8,128)(2,1)} %param.9) | copy-start | bytes 1572868
  227.7 6.2 %copy-start.5 = (bf16[1,512,512]{2,1,0:T(8,128)(2,1)S(1)}, bf16[1,512,512]{2,1,0:T(8,128)(2,1)}, u32[]{:S(2)}) copy-start(bf16[1,512,512]{2,1,0:T(8,128)(2,1)} %param.10) | copy-start | bytes 1572868
  236.3 1.2 copy-start.1
  237.5 44.4 %copy-start.6 = (f32[512,512]{1,0:T(8,128)}, f32[512,512]{1,0:T(8,128)S(1)}, u32[]{:S(2)}) copy-start(f32[512,512]{1,0:T(8,128)S(1)} %convolution_multiply_fusion) | copy-start | bytes 3145732
  238.2 4.5 collective-permute-start
  285.3 4.5 collective-permute-start.1
  328.6 4.5 collective-permute-start.2
  372.0 4.9 collective-permute-start.3
  415.4 6.0 %collective-permute-start.4 = (f32[512,8]{0,1:T(8,128)S(1)}, f32[512,8]{0,1:T(8,128)S(1)}, u32[]{:S(2)}, u32[]{:S(2)}) collective-permute-start(f32[512,8]{0,1:T(8,128)S(1)} %convolution_add_fusion.3), channel_id=1, source_target_pairs={{64,0},{128,64},{192,128},{256,192},{320,256},{384,320},{448,384},... | collective-permute-start | bytes 49160 | tf_op jit(solution)/shard_map/ppermute | solution.py:10
  460.0 6.0 %collective-permute-start.5 = (f32[512,8]{0,1:T(8,128)S(1)}, f32[512,8]{0,1:T(8,128)S(1)}, u32[]{:S(2)}, u32[]{:S(2)}) collective-permute-start(f32[512,8]{0,1:T(8,128)S(1)} %convolution_add_fusion.2), channel_id=1, source_target_pairs={{64,0},{128,64},{192,128},{256,192},{320,256},{384,320},{448,384},... | collective-permute-start | bytes 49160 | tf_op jit(solution)/shard_map/ppermute | solution.py:10
  504.6 6.0 %collective-permute-start.6 = (f32[512,8]{0,1:T(8,128)S(1)}, f32[512,8]{0,1:T(8,128)S(1)}, u32[]{:S(2)}, u32[]{:S(2)}) collective-permute-start(f32[512,8]{0,1:T(8,128)S(1)} %convolution_add_fusion.1), channel_id=1, source_target_pairs={{64,0},{128,64},{192,128},{256,192},{320,256},{384,320},{448,384},... | collective-permute-start | bytes 49160 | tf_op jit(solution)/shard_map/ppermute | solution.py:10
  548.6 3.7 copy-start.3
Sparse Core Ops, SparseCore 0:
  18.7 204.5 all-reduce.2
